TPU v7x, 512 devices: a whole 4x8x8 slice. The times are simulated.
512 devices in a mesh: req: 64 (over z, x, core), tp: 8 (over y).
Axes of the slice: x: 4, y: 8, z: 8, core: 2. Of those that a mesh axis runs over, the one named last changes fastest.
Arguments:
- queries: bfloat16 [1024, 2048], P('req', 'tp'), may hold values from -27 to 27
- fresh_cache: bfloat16 [1024, 2, 2048], P('req', None, 'tp'), may hold values from -4 to 4
- tail_cache: bfloat16 [1024, 32, 2, 2048], P('req', None, None, 'tp'), may hold values from -4 to 4
- tail_len: int32 [1024], P('req'), may hold values from 1 to 32, as said below
- pool_cache: bfloat16 [2048, 64, 2, 2048], P('req', None, None, 'tp'), may hold values from -4 to 4
- page_group: int32 [2048], P('req'), may hold values from 0 to 63, as said below
- page_start: int32 [2048], P('req'), may hold values from 0 to 16320, as said below
- prompt_len: int32 [64], replicated, may hold values from 1 to 16384, as said below
- residual: bfloat16 [1024, 2048], P('req'), may hold values from -80 to 80
- out_weight: bfloat16 [2048, 2048], P('tp'), may hold values from -0.125 to 0.125
- out_bias: bfloat16 [2048], replicated, may hold values from -0.796875 to 0.796875
- norm_gain: bfloat16 [2048], P('tp'), may hold values from 0.5 to 1.5
- norm_shift: bfloat16 [2048], P('tp'), may hold values from -0.796875 to 0.796875
Outputs:
- attention_out: bfloat16 [1024, 2048], P('req', 'tp')
- normed: bfloat16 [1024, 2048], P('req', 'tp')
Inputs may be any that keep to these rules, and one draw needn't show every extreme that they name: page_group[p] is the group whose prompt page p holds; every page holds some group's prompt; every group holds at least one page and at most 256 pages, and some group holds exactly 256; the pages of a group of n pages lie on min(n, 64) different indices of req, none holding more than ceil(n / 64) of them. The pages of a group of n pages have page_start 0, 64, ..., (n - 1) * 64, each once. `prompt_len`: a group of n pages has a prompt of (n - 1) * 64 + 1 to n * 64 positions. `tail_len`: some request has exactly 32 tail positions.
All inputs are finite; a program needn't handle non-finite values.
Results may differ from a plain program's by a relative error of at most 0.02.
Values may be sent and summed in bfloat16 or wider, within the bound.
No kernel may reach another device: no remote copies, remote signals or barrier semaphores. Data moves between devices by JAX's collectives and lax.ppermute only.
A program may use at most 64 MiB of HBM per device.

v0:
```python
import math
import jax
import jax.numpy as jnp
from jax import lax
from jax.sharding import PartitionSpec as P

HEADS = 16
HEAD = 128
PAGE = 64
masked_score = -1e30
norm_epsilon = 1e-05


def split_halves(values):
    upper_part = lax.optimization_barrier(values.astype(jnp.bfloat16))
    lower_part = (values - upper_part.astype(jnp.float32)).astype(jnp.bfloat16)
    return (upper_part, lower_part)


def local(
    queries,
    fresh_cache,
    tail_cache,
    tail_len,
    pool_cache,
    page_group,
    page_start,
    prompt_len,
    residual,
    out_weight,
    out_bias,
    norm_gain,
    norm_shift,
):
    f32 = jnp.float32
    highest = lax.Precision.HIGHEST
    row_count, feat_width = queries.shape
    heads_here = feat_width // HEAD
    inv_root = 1.0 / math.sqrt(HEAD)
    head_ids = lax.axis_index("tp") * heads_here + jnp.arange(heads_here)
    slopes = jnp.exp2(-8.0 * (head_ids.astype(f32) + 1.0) / HEADS)
    group_count = prompt_len.shape[0]
    page_count = pool_cache.shape[0]
    tail_slots = tail_cache.shape[1]
    n_req = lax.axis_size("req")
    assert group_count == n_req
    everyone = lax.all_gather(queries, "req", axis=0, tiled=True)
    by_group = everyone.reshape(group_count, row_count, heads_here, HEAD)
    safe_group = jnp.clip(page_group, 0, group_count - 1)
    page_queries = by_group[safe_group]
    page_keys = pool_cache[:, :, 0].reshape(page_count, PAGE, heads_here, HEAD)
    page_values = pool_cache[:, :, 1].reshape(page_count, PAGE, heads_here, HEAD)
    prompt_here = prompt_len[safe_group]
    positions = page_start[:, None] + jnp.arange(PAGE)[None, :]
    usable = (positions < prompt_here[:, None]) & (page_group[:, None] >= 0)
    offsets = (positions - prompt_here[:, None]).astype(f32)
    scores = (
        jnp.einsum("pqhd,pshd->pqhs", page_queries, page_keys, preferred_element_type=f32)
        * inv_root
    )
    scores = scores + slopes[None, None, :, None] * offsets[:, None, None, :]
    scores = jnp.where(usable[:, None, None, :], scores, masked_score)
    member = (page_group[:, None] == jnp.arange(group_count)[None, :]) & (page_group[:, None] >= 0)
    page_top = scores.max(-1)
    local_top = jnp.where(member[:, :, None, None], page_top[:, None], masked_score).max(0)
    page_ref = local_top[safe_group]
    weights = jnp.where(usable[:, None, None, :], jnp.exp(scores - page_ref[..., None]), 0.0)
    page_totals = weights.sum(-1)
    upper_part, lower_part = split_halves(weights)
    page_accum = jnp.einsum("pqhs,pshd->pqhd", upper_part, page_values, preferred_element_type=f32)
    page_accum = page_accum + jnp.einsum(
        "pqhs,pshd->pqhd", lower_part, page_values, preferred_element_type=f32
    )
    accum_upper, accum_lower = split_halves(page_accum.reshape(page_count, -1))
    spread = member.T.astype(jnp.bfloat16)
    group_accum = jnp.dot(spread, accum_upper, preferred_element_type=f32)
    group_accum = group_accum + jnp.dot(spread, accum_lower, preferred_element_type=f32)
    group_totals = jnp.dot(
        member.T.astype(f32), page_totals.reshape(page_count, -1), precision=highest
    )
    stats_width = row_count * heads_here
    pad_width = -(group_accum.shape[1] + 2 * stats_width) % 128
    packed = jnp.concatenate(
        [
            group_accum,
            local_top.reshape(group_count, stats_width),
            group_totals,
            jnp.zeros((group_count, pad_width), f32),
        ],
        axis=1,
    )
    arrived = lax.all_to_all(packed, "req", 0, 0, tiled=True)
    accum_width = row_count * feat_width
    part_accum = arrived[:, :accum_width].reshape(n_req, row_count, heads_here, HEAD)
    part_top = arrived[:, accum_width : accum_width + stats_width].reshape(
        n_req, row_count, heads_here
    )
    part_totals = arrived[:, accum_width + stats_width : accum_width + 2 * stats_width].reshape(
        n_req, row_count, heads_here
    )
    home_queries = queries.reshape(row_count, heads_here, HEAD)
    tail_keys = tail_cache[:, :, 0].reshape(row_count, tail_slots, heads_here, HEAD)
    tail_values = tail_cache[:, :, 1].reshape(row_count, tail_slots, heads_here, HEAD)
    fresh_keys = fresh_cache[:, 0].reshape(row_count, heads_here, HEAD)
    fresh_values = fresh_cache[:, 1].reshape(row_count, heads_here, HEAD)
    slot_ids = jnp.arange(tail_slots)
    tail_scores = (
        jnp.einsum("qhd,qjhd->qhj", home_queries, tail_keys, preferred_element_type=f32) * inv_root
    )
    tail_scores = tail_scores + slopes[None, :, None] * slot_ids.astype(f32)[None, None, :]
    tail_scores = jnp.where(
        slot_ids[None, None, :] < tail_len[:, None, None], tail_scores, masked_score
    )
    own_scores = (
        jnp.einsum("qhd,qhd->qh", home_queries, fresh_keys, preferred_element_type=f32) * inv_root
    )
    own_scores = own_scores + slopes[None, :] * tail_len.astype(f32)[:, None]
    home_top = jnp.maximum(tail_scores.max(-1), own_scores)
    row_top = jnp.maximum(home_top, part_top.max(0))
    part_scale = jnp.exp(part_top - row_top[None])
    pool_totals = jnp.sum(part_scale * part_totals, 0)
    pool_accum = jnp.sum(part_scale[..., None] * part_accum, 0)
    tail_weights = jnp.exp(tail_scores - row_top[:, :, None])
    own_weights = jnp.exp(own_scores - row_top)
    totals = tail_weights.sum(-1) + own_weights
    upper_part, lower_part = split_halves(tail_weights)
    accum = jnp.einsum("qhj,qjhd->qhd", upper_part, tail_values, preferred_element_type=f32)
    accum = accum + jnp.einsum("qhj,qjhd->qhd", lower_part, tail_values, preferred_element_type=f32)
    home_accum = accum + own_weights[:, :, None] * fresh_values.astype(f32)
    attention = ((pool_accum + home_accum) / (pool_totals + totals)[:, :, None]).astype(
        jnp.bfloat16
    )
    attention = attention.reshape(row_count, feat_width)
    partial_value = jnp.dot(attention, out_weight, preferred_element_type=f32)
    model_width = residual.shape[1]
    own_start = lax.axis_index("tp") * feat_width
    summed = lax.psum_scatter(
        partial_value.astype(jnp.bfloat16), "tp", scatter_dimension=1, tiled=True
    ).astype(jnp.float32)
    bias_mine = lax.dynamic_slice_in_dim(out_bias, own_start, feat_width, 0).astype(f32)
    attention_mine = (summed + bias_mine[None, :]).astype(jnp.bfloat16)
    residual_mine = lax.dynamic_slice_in_dim(residual, own_start, feat_width, 1).astype(f32)
    hidden_mine = residual_mine + attention_mine.astype(f32)
    first_sum, second_sum = lax.psum(
        (jnp.sum(hidden_mine, -1), jnp.sum(hidden_mine * hidden_mine, -1)), "tp"
    )
    row_mean = (first_sum / model_width)[:, None]
    mean_square = (second_sum / model_width)[:, None]
    row_var = mean_square - row_mean * row_mean
    normed = (
        (hidden_mine - row_mean)
        * lax.rsqrt(row_var + norm_epsilon)
        * norm_gain.astype(f32)[None, :]
    )
    normed = normed + norm_shift.astype(f32)[None, :]
    return (attention_mine, normed.astype(jnp.bfloat16))


def solution(mesh):
    in_specs = (
        P("req", "tp"),
        P("req", None, "tp"),
        P("req", None, None, "tp"),
        P("req"),
        P("req", None, None, "tp"),
        P("req"),
        P("req"),
        P(),
        P("req", None),
        P("tp", None),
        P(),
        P("tp"),
        P("tp"),
    )
    out_specs = (P("req", "tp"), P("req", "tp"))
    return jax.shard_map(local, mesh=mesh, in_specs=in_specs, out_specs=out_specs, check_vma=False)
```

profile of v0, /device:TPU:2, one launch (start us, length us, event | category | flops | bytes accessed | tf_op | source)
XLA Modules:
  0.0 193.3 jit_solution(1942544731091071462)
XLA Ops:
  7.2 0.7 compare_select_fusion
  7.9 0.7 broadcast_compare_fusion
  8.6 1.4 gather_fusion
  10.0 0.7 subtract_convert_fusion.5
  10.7 0.8 fusion.33
  11.5 56.0 %all_gather.3 = bf16[1024,256]{1,0:T(8,128)(2,1)S(1)} all-gather(bf16[16,256]{1,0:T(8,128)(2,1)} %param.13), channel_id=1, replica_groups=mesh['req'=64,'tp'=8] {'req'}, dimensions={0}, use_global_device_ids=true | all-gather | bytes 532480 | tf_op jit(solution)/shard_map/all_gather | solution.py:47
  67.7 0.6 gather_fusion.1
  68.3 10.7 %slice_reduce_fusion = (bf16[32,64,256]{2,1,0:T(8,128)(2,1)S(1)}, bf16[32,64,256]{2,1,0:T(8,128)(2,1)S(1)}) fusion(bf16[32,64,2,256]{3,2,1,0:T(2,128)(2,1)} %param.17), kind=kLoop, calls=%fused_computation.7 | loop fusion | bytes 4194304 | tf_op jit(solution)/shard_map/slice | solution.py:52
  79.1 0.8 fusion.50
  80.2 0.6 gather_fusion.2
  80.8 0.4 fusion.12
  81.6 0.5 fusion.1
  84.5 2.1 %copy.57 = f32[64,1,4224]{2,1,0:T(1,128)} copy(f32[64,1,4224]{2,0,1:T(8,128)S(1)} %bitcast.87) | data formatting | bytes 2162688 | tf_op jit(solution)/shard_map/all_to_all | solution.py:92
  86.6 6.3 %all-to-all-start = ((f32[64,1,4224]{2,1,0:T(1,128)}), f32[64,1,4224]{2,1,0:T(1,128)}, u32[]{:S(2)}, u32[]{:S(2)}) async-start(f32[64,1,4224]{2,1,0:T(1,128)} %copy.57), calls=%async_computation | async-start | bytes 2162688 | tf_op jit(solution)/shard_map/all_to_all | solution.py:92
  93.7 2.2 %slice_reduce_fusion.2 = (bf16[16,32,256]{2,1,0:T(8,128)(2,1)S(1)}, bf16[16,32,256]{2,1,0:T(8,128)(2,1)S(1)}) fusion(bf16[16,32,2,256]{3,2,1,0:T(2,128)(2,1)S(1)} %copy-done.1), kind=kLoop, calls=%fused_computation.22 | loop fusion | bytes 1048576 | tf_op jit(solution)/shard_map/slice | solution.py:103
  96.2 26.2 %all-to-all-done = f32[64,1,4224]{2,1,0:T(1,128)} async-done(((f32[64,1,4224]{2,1,0:T(1,128)}), f32[64,1,4224]{2,1,0:T(1,128)}, u32[]{:S(2)}, u32[]{:S(2)}) %all-to-all-start) | async-done | bytes 1081376 | tf_op jit(solution)/shard_map/all_to_all | solution.py:92
  122.4 3.1 %copy.58 = f32[64,1,4224]{0,2,1:T(8,128)S(1)} copy(f32[64,1,4224]{2,1,0:T(1,128)} %all-to-all-done) | data formatting | bytes 2162688 | tf_op jit(solution)/shard_map/all_to_all | solution.py:92
  126.3 0.7 fusion.26
  127.0 0.7 reduce_sum.62
  127.7 0.6 copy.63
  128.4 1.3 add_add_fusion
  129.7 0.8 copy.61
  130.5 0.8 copy.64
  131.7 0.6 fusion
  132.4 0.9 convolution_convert_fusion
  133.3 0.7 convert_element_type.119
  134.0 0.7 convert_element_type.120
  134.7 0.8 dynamic-slice_convert_fusion
  135.4 33.2 %reduce-scatter.2.cloned.1.call-done = bf16[16,256]{1,0:T(8,128)(2,1)} async-done(((bf16[16,2048]{1,0:T(8,128)(2,1)}), bf16[16,256]{1,0:T(8,128)(2,1)}) %reduce-scatter.2.cloned.1.call-update) | async-done | bytes 8208 | tf_op jit(solution)/shard_map/reduce_scatter | solution.py:137
  168.6 0.8 fusion.36
  169.4 15.6 %all-reduce = (f32[16]{0:T(128)S(1)}, f32[16]{0:T(128)S(1)}) all-reduce(f32[16]{0:T(128)S(1)} %get-tuple-element.7, f32[16]{0:T(128)S(1)} %get-tuple-element.6), channel_id=1, replica_groups=mesh['req'=64,'tp'=8] {'tp'}, use_global_device_ids=true, to_apply=%region_12.13 | all-reduce | flops 32 | bytes 256 | tf_op jit(solution)/shard_map/psum | solution.py:144
  185.0 1.4 add_convert_fusion
  (62 shorter events, 5.6 us)
Async XLA Ops:
  7.2 125.3 %copy-start = (bf16[256,2048]{1,0:T(8,128)(2,1)S(1)}, bf16[256,2048]{1,0:T(8,128)(2,1)}, u32[]{:S(2)}) copy-start(bf16[256,2048]{1,0:T(8,128)(2,1)} %param.22) | copy-start | bytes 3145732
  82.1 0.8 copy-start.5
  84.4 8.8 %copy-start.2 = (bf16[16,256]{1,0:T(8,128)(2,1)S(1)}, bf16[16,256]{1,0:T(8,128)(2,1)}, u32[]{:S(2)}) copy-start(bf16[16,256]{1,0:T(8,128)(2,1)} %param.13) | copy-start | bytes 24580
  84.4 8.8 %copy-start.3 = (bf16[16,2,256]{2,1,0:T(2,128)(2,1)S(1)}, bf16[16,2,256]{2,1,0:T(2,128)(2,1)}, u32[]{:S(2)}) copy-start(bf16[16,2,256]{2,1,0:T(2,128)(2,1)} %param.14) | copy-start | bytes 49156
  84.4 9.1 %copy-start.7 = (s32[16]{0:T(128)S(1)}, s32[16]{0:T(128)}, u32[]{:S(2)}) copy-start(s32[16]{0:T(128)} %param.16) | copy-start | bytes 196
  84.5 9.2 %copy-start.1 = (bf16[16,32,2,256]{3,2,1,0:T(2,128)(2,1)S(1)}, bf16[16,32,2,256]{3,2,1,0:T(2,128)(2,1)}, u32[]{:S(2)}) copy-start(bf16[16,32,2,256]{3,2,1,0:T(2,128)(2,1)} %param.15) | copy-start | bytes 1572868
  86.6 35.8 %all-to-all-start = ((f32[64,1,4224]{2,1,0:T(1,128)}), f32[64,1,4224]{2,1,0:T(1,128)}, u32[]{:S(2)}, u32[]{:S(2)}) async-start(f32[64,1,4224]{2,1,0:T(1,128)} %copy.57), calls=%async_computation | async-start | bytes 2162688 | tf_op jit(solution)/shard_map/all_to_all | solution.py:92
  93.0 75.6 %reduce-scatter.2.cloned.1.call-start = ((), (), s32[]{:S(2)}) async-start(), calls=%async_computation.2 | async-start | bytes 73728 | tf_op jit(solution)/shard_map/reduce_scatter | solution.py:137
  93.5 32.3 %copy-start.6 = (f32[16]{0:T(128)}, f32[16]{0:T(128)S(1)}, u32[]{:S(2)}) copy-start(f32[16]{0:T(128)S(1)} %convert_element_type.106) | copy-start | bytes 196
  169.4 17.0 %copy-start.4 = (bf16[16,256]{1,0:T(8,128)(2,1)}, bf16[16,256]{1,0:T(8,128)(2,1)S(1)}, u32[]{:S(2)}) copy-start(bf16[16,256]{1,0:T(8,128)(2,1)S(1)} %get-tuple-element.10) | copy-start | bytes 24580
Sparse Core Ops, SparseCore 0:
  133.5 35.0 reduce-scatter.1
where the time goes:
time: 194 us; the launch traced here: 193 us
  blocking collectives  71.6 us (37%)
  waiting for transfers between devices  59.4 us (31%)
  local copies, waits for them, and re-layouts  25.5 us (13%)
  between operations  14.3 us (7%)
  other arithmetic  11.6 us (6%)
  starting transfers between devices  6.56 us (3%)
  matrix products  4.23 us (2%)
    all_gather x1, blocking collectives, local(): everyone = lax.all_gather(queries, 'req', axis=0, tiled=True)  56 us
    reduce_scatter x1, waiting for transfers between devices, local(): lax.psum_scatter(partial_value.astype(jnp.bfloat16), 'tp', scatter_dimens...  33.2 us
    all_to_all x1, waiting for transfers between devices, local(): arrived = lax.all_to_all(packed, 'req', 0, 0, tiled=True)  26.2 us
    psum x1, blocking collectives, local(): lax.psum((jnp.sum(hidden_mine, -1), jnp.sum(hidden_mine * hidden_mine, -1...  15.6 us
    slice x1, local copies, waits for them, and re-layouts, local(): pool_cache[:, :, 1].reshape(page_count, PAGE, heads_here, HEAD)  10.7 us
    all_to_all x1, starting transfers between devices, local(): arrived = lax.all_to_all(packed, 'req', 0, 0, tiled=True)  6.34 us
    all_to_all x2, local copies, waits for them, and re-layouts, local(): arrived = lax.all_to_all(packed, 'req', 0, 0, tiled=True)  5.25 us
  transfers between devices with their start and end apart: 2, of which 2 were waited for; matrix products, arithmetic and copies ran while one was open for 3% of the time, Pallas kernels for 0%

commit v1 on v0

--- a/solution.py
+++ b/solution.py
@@ -1,3 +1,4 @@
+import functools
 import math
 import jax
 import jax.numpy as jnp
@@ -9,6 +10,21 @@
 PAGE = 64
 masked_score = -1e30
 norm_epsilon = 1e-05
+
+
+def settle_roads(raw, d0):
+    return jnp.concatenate(
+        lax.all_to_all(
+            jnp.stack([raw for _ in range(lax.axis_size("req"))], 0),
+            split_axis=0,
+            axis_name="req",
+            concat_axis=0,
+        ),
+        axis=d0,
+    )
+
+
+target_move = functools.partial(settle_roads, d0=0)
 
 
 def split_halves(values):
@@ -44,7 +60,7 @@
     tail_slots = tail_cache.shape[1]
     n_req = lax.axis_size("req")
     assert group_count == n_req
-    everyone = lax.all_gather(queries, "req", axis=0, tiled=True)
+    everyone = target_move(queries)
     by_group = everyone.reshape(group_count, row_count, heads_here, HEAD)
     safe_group = jnp.clip(page_group, 0, group_count - 1)
     page_queries = by_group[safe_group]

time: 194 us -> 158 us (0.81)
  blocking collectives: 71.6 us -> 15.6 us
  starting transfers between devices: 6.56 us -> 21.6 us
  waiting for transfers between devices: 59.4 us -> 62.3 us
  local copies, waits for them, and re-layouts: 25.5 us -> 28 us
    all_gather x1 -> x0, blocking collectives: 56 us -> none  [local(): everyone = lax.all_gather(queries, 'req', axis=0, tiled=True)]
    all_to_all x0 -> x1, starting transfers between devices: none -> 13.9 us  [settle_roads(): lax.all_to_all(jnp.stack([raw for _ in range(lax.axis_size('req'))], 0),...]
    all_to_all x0 -> x1, waiting for transfers between devices: none -> 2.93 us  [settle_roads(): lax.all_to_all(jnp.stack([raw for _ in range(lax.axis_size('req'))], 0),...]
  transfers between devices with their start and end apart: 2 -> 3, of which waited for: 2 -> 3; matrix products, arithmetic and copies ran while one was open for 3% -> 12% of each run, Pallas kernels for 0% -> 0%
where the time goes in v1:
time: 158 us
  waiting for transfers between devices  62.3 us (39%)
  local copies, waits for them, and re-layouts  28 us (18%)
  starting transfers between devices  21.6 us (14%)
  blocking collectives  15.6 us (10%)
  between operations  14.3 us (9%)
  other arithmetic  10.2 us (6%)
  matrix products  5.47 us (3%)
    reduce_scatter x1, waiting for transfers between devices, local(): lax.psum_scatter(partial_value.astype(jnp.bfloat16), 'tp', scatter_dimens...  33.2 us
    all_to_all x1, waiting for transfers between devices, local(): arrived = lax.all_to_all(packed, 'req', 0, 0, tiled=True)  26.2 us
    psum x1, blocking collectives, local(): lax.psum((jnp.sum(hidden_mine, -1), jnp.sum(hidden_mine * hidden_mine, -1...  15.6 us
    all_to_all x1, starting transfers between devices, settle_roads(): lax.all_to_all(jnp.stack([raw for _ in range(lax.axis_size('req'))], 0),...  13.9 us
    slice x1, local copies, waits for them, and re-layouts, local(): pool_cache[:, :, 1].reshape(page_count, PAGE, heads_here, HEAD)  11.7 us
    all_to_all x1, starting transfers between devices, local(): arrived = lax.all_to_all(packed, 'req', 0, 0, tiled=True)  7.53 us
    all_to_all x2, local copies, waits for them, and re-layouts, local(): arrived = lax.all_to_all(packed, 'req', 0, 0, tiled=True)  5.25 us
  transfers between devices with their start and end apart: 3, of which 3 were waited for; matrix products, arithmetic and copies ran while one was open for 12% of the time, Pallas kernels for 0%

profile of v1, /device:TPU:2, one launch (start us, length us, event | category | flops | bytes accessed | tf_op | source)
XLA Modules:
  0.0 157.5 jit_solution(1046885522118408697)
XLA Ops:
  7.2 1.6 %stack.2 = bf16[64,16,256]{2,1,0:T(8,128)(2,1)} broadcast(bf16[16,256]{1,0:T(8,128)(2,1)} %param.13), dimensions={1,2} | broadcast | bytes 532480 | tf_op jit(solution)/shard_map/stack | solution.py:18
  8.8 13.9 %all-to-all-start = ((bf16[64,16,256]{2,1,0:T(8,128)(2,1)}), bf16[64,16,256]{2,1,0:T(8,128)(2,1)S(1)}, u32[]{:S(2)}, u32[]{:S(2)}) async-start(bf16[64,16,256]{2,1,0:T(8,128)(2,1)} %stack.2), calls=%async_computation | async-start | bytes 1048576 | tf_op jit(solution)/shard_map/all_to_all | solution.py:17
  22.7 0.7 compare_select_fusion
  23.4 0.7 broadcast_compare_fusion
  24.1 1.4 gather_fusion
  25.7 11.7 %slice_reduce_fusion = (bf16[32,64,256]{2,1,0:T(8,128)(2,1)S(1)}, bf16[32,64,256]{2,1,0:T(8,128)(2,1)}) fusion(bf16[32,64,2,256]{3,2,1,0:T(2,128)(2,1)} %param.17), kind=kLoop, calls=%fused_computation.7 | loop fusion | bytes 4194304 | tf_op jit(solution)/shard_map/slice | solution.py:68
  37.3 2.9 %all-to-all-done = bf16[64,16,256]{2,1,0:T(8,128)(2,1)S(1)} async-done(((bf16[64,16,256]{2,1,0:T(8,128)(2,1)}), bf16[64,16,256]{2,1,0:T(8,128)(2,1)S(1)}, u32[]{:S(2)}, u32[]{:S(2)}) %all-to-all-start) | async-done | bytes 524320 | tf_op jit(solution)/shard_map/all_to_all | solution.py:17
  40.4 0.6 gather_fusion.1
  41.0 2.0 %fusion.50 = (f32[32,16,2]{1,2,0:T(2,128)S(1)}, f32[32,16,2,64]{3,1,2,0:T(8,128)S(1)}) fusion(f32[32,2,64]{2,1,0:T(2,128)S(1)} %broadcast_multiply_fusion, bf16[32,16,2,128]{3,1,2,0:T(8,128)(2,1)S(1)} %gather_fusion.1, pred[32,64]{1,0:T(8,128)(4,1)S(1)} %get-tuple-element.24, bf16[32,64,256]{2,1,0:T(8,128)(2,1)} %get-tuple-element.3), kind=kOutput, calls=%fused_computation.96 | convolution fusion | flops 17038336 | bytes 1595392 | tf_op jit(solution)/shard_map/pqhd,pshd->pqhs/dot_general | solution.py:74
  43.3 0.6 gather_fusion.2
  43.9 0.4 fusion.12
  44.7 0.5 fusion.1
  47.6 2.1 %copy.57 = f32[64,1,4224]{2,1,0:T(1,128)} copy(f32[64,1,4224]{2,0,1:T(8,128)S(1)} %bitcast.92) | data formatting | bytes 2162688 | tf_op jit(solution)/shard_map/all_to_all | solution.py:108
  49.7 7.5 %all-to-all-start.1 = ((f32[64,1,4224]{2,1,0:T(1,128)}), f32[64,1,4224]{2,1,0:T(1,128)}, u32[]{:S(2)}, u32[]{:S(2)}) async-start(f32[64,1,4224]{2,1,0:T(1,128)} %copy.57), calls=%async_computation.1 | async-start | bytes 2162688 | tf_op jit(solution)/shard_map/all_to_all | solution.py:108
  58.0 2.2 %slice_reduce_fusion.2 = (bf16[16,32,256]{2,1,0:T(8,128)(2,1)S(1)}, bf16[16,32,256]{2,1,0:T(8,128)(2,1)S(1)}) fusion(bf16[16,32,2,256]{3,2,1,0:T(2,128)(2,1)S(1)} %copy-done.1), kind=kLoop, calls=%fused_computation.23 | loop fusion | bytes 1048576 | tf_op jit(solution)/shard_map/slice | solution.py:119
  60.5 26.2 %all-to-all-done.1 = f32[64,1,4224]{2,1,0:T(1,128)} async-done(((f32[64,1,4224]{2,1,0:T(1,128)}), f32[64,1,4224]{2,1,0:T(1,128)}, u32[]{:S(2)}, u32[]{:S(2)}) %all-to-all-start.1) | async-done | bytes 1081376 | tf_op jit(solution)/shard_map/all_to_all | solution.py:108
  86.7 3.1 %copy.58 = f32[64,1,4224]{0,2,1:T(8,128)S(1)} copy(f32[64,1,4224]{2,1,0:T(1,128)} %all-to-all-done.1) | data formatting | bytes 2162688 | tf_op jit(solution)/shard_map/all_to_all | solution.py:108
  90.6 0.7 fusion.26
  91.3 0.7 reduce_sum.62
  92.0 0.6 copy.63
  92.7 1.3 add_add_fusion
  94.0 0.8 copy.61
  94.8 0.8 copy.64
  96.0 0.6 fusion
  96.7 0.9 convolution_convert_fusion
  97.6 0.7 convert_element_type.119
  98.3 0.7 convert_element_type.120
  99.0 0.8 dynamic-slice_convert_fusion
  99.7 33.2 %reduce-scatter.2.cloned.1.call-done = bf16[16,256]{1,0:T(8,128)(2,1)} async-done(((bf16[16,2048]{1,0:T(8,128)(2,1)}), bf16[16,256]{1,0:T(8,128)(2,1)}) %reduce-scatter.2.cloned.1.call-update) | async-done | bytes 8208 | tf_op jit(solution)/shard_map/reduce_scatter | solution.py:153
  132.9 0.8 fusion.36
  133.7 15.6 %all-reduce = (f32[16]{0:T(128)S(1)}, f32[16]{0:T(128)S(1)}) all-reduce(f32[16]{0:T(128)S(1)} %get-tuple-element.7, f32[16]{0:T(128)S(1)} %get-tuple-element.6), channel_id=1, replica_groups=mesh['req'=64,'tp'=8] {'tp'}, use_global_device_ids=true, to_apply=%region_12.13 | all-reduce | flops 32 | bytes 256 | tf_op jit(solution)/shard_map/psum | solution.py:160
  149.3 1.4 add_convert_fusion
  (65 shorter events, 5.7 us)
Async XLA Ops:
  7.2 89.6 %copy-start = (bf16[256,2048]{1,0:T(8,128)(2,1)S(1)}, bf16[256,2048]{1,0:T(8,128)(2,1)}, u32[]{:S(2)}) copy-start(bf16[256,2048]{1,0:T(8,128)(2,1)} %param.22) | copy-start | bytes 3145732
  7.2 18.3 %copy-start.5 = (s32[32]{0:T(128)S(1)}, s32[32]{0:T(128)}, u32[]{:S(2)}) copy-start(s32[32]{0:T(128)} %param.18) | copy-start | bytes 388
  7.2 18.2 %copy-start.7 = (s32[32]{0:T(128)S(1)}, s32[32]{0:T(128)}, u32[]{:S(2)}) copy-start(s32[32]{0:T(128)} %param.19) | copy-start | bytes 388
  8.8 31.4 %all-to-all-start = ((bf16[64,16,256]{2,1,0:T(8,128)(2,1)}), bf16[64,16,256]{2,1,0:T(8,128)(2,1)S(1)}, u32[]{:S(2)}, u32[]{:S(2)}) async-start(bf16[64,16,256]{2,1,0:T(8,128)(2,1)} %stack.2), calls=%async_computation | async-start | bytes 1048576 | tf_op jit(solution)/shard_map/all_to_all | solution.py:17
  47.5 9.9 %copy-start.2 = (bf16[16,256]{1,0:T(8,128)(2,1)S(1)}, bf16[16,256]{1,0:T(8,128)(2,1)}, u32[]{:S(2)}) copy-start(bf16[16,256]{1,0:T(8,128)(2,1)} %param.13) | copy-start | bytes 24580
  47.5 10.0 %copy-start.3 = (bf16[16,2,256]{2,1,0:T(2,128)(2,1)S(1)}, bf16[16,2,256]{2,1,0:T(2,128)(2,1)}, u32[]{:S(2)}) copy-start(bf16[16,2,256]{2,1,0:T(2,128)(2,1)} %param.14) | copy-start | bytes 49156
  47.6 10.2 %copy-start.8 = (s32[16]{0:T(128)S(1)}, s32[16]{0:T(128)}, u32[]{:S(2)}) copy-start(s32[16]{0:T(128)} %param.16) | copy-start | bytes 196
  47.6 10.4 %copy-start.1 = (bf16[16,32,2,256]{3,2,1,0:T(2,128)(2,1)S(1)}, bf16[16,32,2,256]{3,2,1,0:T(2,128)(2,1)}, u32[]{:S(2)}) copy-start(bf16[16,32,2,256]{3,2,1,0:T(2,128)(2,1)} %param.15) | copy-start | bytes 1572868
  49.7 37.0 %all-to-all-start.1 = ((f32[64,1,4224]{2,1,0:T(1,128)}), f32[64,1,4224]{2,1,0:T(1,128)}, u32[]{:S(2)}, u32[]{:S(2)}) async-start(f32[64,1,4224]{2,1,0:T(1,128)} %copy.57), calls=%async_computation.1 | async-start | bytes 2162688 | tf_op jit(solution)/shard_map/all_to_all | solution.py:108
  57.3 75.6 %reduce-scatter.2.cloned.1.call-start = ((), (), s32[]{:S(2)}) async-start(), calls=%async_computation.3 | async-start | bytes 73728 | tf_op jit(solution)/shard_map/reduce_scatter | solution.py:153
  57.8 32.3 %copy-start.6 = (f32[16]{0:T(128)}, f32[16]{0:T(128)S(1)}, u32[]{:S(2)}) copy-start(f32[16]{0:T(128)S(1)} %convert_element_type.106) | copy-start | bytes 196
  133.7 17.0 %copy-start.4 = (bf16[16,256]{1,0:T(8,128)(2,1)}, bf16[16,256]{1,0:T(8,128)(2,1)S(1)}, u32[]{:S(2)}) copy-start(bf16[16,256]{1,0:T(8,128)(2,1)S(1)} %get-tuple-element.10) | copy-start | bytes 24580
Sparse Core Ops, SparseCore 0:
  97.8 35.0 reduce-scatter.1
